TPU v7x, 512 devices: a whole 4x4x16 slice. The times are simulated.
512 devices in a mesh: fsdp: 128 (over z, y, core), seq: 4 (over x).
Axes of the slice: x: 4, y: 4, z: 16, core: 2. Of those that a mesh axis runs over, the one named last changes fastest.
Arguments:
- tokens: bfloat16 [128, 512, 8192], P('fsdp', 'seq'), may hold values from -6 to 6
- queries: bfloat16 [128, 512, 8192], P('fsdp', None, 'seq'), may hold values from -6 to 6
- key_weight: bfloat16 [8192, 1024], P('fsdp', 'seq'), may hold values from -1 to 1
- u_factor: float32 [8192, 64], P('fsdp'), may hold values from -6 to 6
- v_factor: float32 [1024, 64], replicated, may hold values from -6 to 6
Outputs:
- update: float32 [8192, 1024], P('fsdp')
- losses: float32 [2], replicated
All inputs are finite; a program needn't handle non-finite values.
Results may differ from a plain program's by a relative error of at most 0.0003.
Values may be sent and summed in bfloat16 or wider, within the bound.
No kernel may reach another device: no remote copies, remote signals or barrier semaphores. Data moves between devices by JAX's collectives and lax.ppermute only.
A program may use at most 64 MiB of HBM per device.

v0:
```python
import math
import jax
import jax.numpy as jnp
from jax import lax
from jax.sharding import PartitionSpec as P

D = 8192
HQ = 64
HD = 128
R = 64
KD = 1024
GROUP = 8


def highest(left, right):
    return jnp.dot(left, right, precision=lax.Precision.HIGHEST, preferred_element_type=jnp.float32)


def solve_rows(rows, gram):
    lower = jnp.linalg.cholesky(gram)
    return lax.linalg.triangular_solve(lower, rows, left_side=False, lower=True, transpose_a=True)


def local(tokens, queries, key_weight, u_factor, v_factor):
    q_v = v_factor
    for turn in range(2):
        q_v = solve_rows(q_v, highest(q_v.T, q_v))
    u_rows = u_factor
    for turn in range(2):
        whole_u = lax.all_gather(u_rows, "fsdp", axis=0, tiled=True)
        u_rows = solve_rows(u_rows, highest(whole_u.T, whole_u))
    q_low = u_rows.astype(jnp.bfloat16)
    whole_x = lax.all_gather(tokens, "seq", axis=1, tiled=True)[0]
    length = whole_x.shape[0]
    slice_width = key_weight.shape[1]
    weight_piece = lax.all_gather(key_weight, "fsdp", axis=0, tiled=True)
    factor_piece = lax.all_gather(q_low, "fsdp", axis=0, tiled=True)
    base = jnp.dot(whole_x, weight_piece, preferred_element_type=jnp.float32)
    side = jnp.dot(whole_x, factor_piece, preferred_element_type=jnp.float32)
    col_start = lax.axis_index("seq") * slice_width
    v_slice = lax.dynamic_slice_in_dim(q_v, col_start, slice_width, 0)
    offset = 2.0 * highest(side, v_slice.T)
    keys = jnp.stack([base + offset, base - offset]).astype(jnp.bfloat16)
    local_kv = slice_width // HD
    query_rows = queries[0]
    query_heads = query_rows.reshape(length, local_kv, GROUP, HD).transpose(1, 2, 0, 3)
    key_heads = keys.reshape(2, length, local_kv, HD).transpose(2, 0, 1, 3)
    places = jnp.arange(length)
    causal = places[:, None] >= places[None, :]
    factor_scale = 1.0 / math.sqrt(HD)

    def one_query_head(query_one, key_one):
        scores = (
            jnp.einsum("td,npd->ntp", query_one, key_one, preferred_element_type=jnp.float32)
            * factor_scale
        )
        scores = jnp.where(causal[None], scores, -1e30)
        top = jnp.max(scores, axis=-1)
        total = jnp.sum(jnp.where(causal[None], jnp.exp(scores - top[..., None]), 0.0), axis=-1)
        return jnp.sum(top + jnp.log(total), axis=1)

    def one_key_head(pair):
        group_queries, key_one = pair
        return jnp.sum(
            lax.map(lambda query_one: one_query_head(query_one, key_one), group_queries), axis=0
        )

    partial_sums = jnp.sum(lax.map(one_key_head, (query_heads, key_heads)), axis=0)
    sums = lax.psum(partial_sums, ("fsdp", "seq"))
    losses = sums / (lax.axis_size("fsdp") * length * HQ)
    unit = math.sqrt(D * KD / R)
    update = unit * highest(u_rows, q_v.T)
    return (update, losses)


def solution(mesh):
    in_specs = (
        P("fsdp", "seq", None),
        P("fsdp", None, "seq"),
        P("fsdp", "seq"),
        P("fsdp", None),
        P(),
    )
    out_specs = (P("fsdp", None), P())
    return jax.shard_map(local, mesh=mesh, in_specs=in_specs, out_specs=out_specs, check_vma=False)
```

profile of v0, /device:TPU:1, one launch (start us, length us, event | category | flops | bytes accessed | tf_op | source)
XLA Modules:
  0.0 858.6 jit_solution(16340279235827252313)
XLA Ops:
  8.0 151.0 %all-gather.6.cloned.1.call-done = f32[8192,64]{1,0:T(8,128)} async-done(((f32[64,64]{1,0:T(8,128)}), f32[8192,64]{1,0:T(8,128)}) %all-gather.6.cloned.1.call-update) | async-done | bytes 2097168 | tf_op jit(solution)/shard_map/all_gather | solution.py:30
  159.0 10.4 %fusion.30 = f32[64,64]{1,0:T(8,128)S(1)} fusion(f32[8192,64]{1,0:T(8,128)} %all-gather.6.cloned.1.call-done), kind=kOutput, calls=%fused_computation.63 | convolution fusion | flops 402653184 | bytes 2113536 | tf_op jit(solution)/shard_map/dot_general | solution.py:16
  169.5 5.8 cholesky.74
  176.7 4.9 custom-call.10
  182.8 137.7 %all-gather.8.cloned.1.call-done = f32[8192,64]{1,0:T(8,128)} async-done(((f32[64,64]{1,0:T(8,128)}), f32[8192,64]{1,0:T(8,128)}) %all-gather.8.cloned.1.call-update) | async-done | bytes 2097168 | tf_op jit(solution)/shard_map/all_gather | solution.py:30
  320.6 10.4 %fusion.31 = f32[64,64]{1,0:T(8,128)S(1)} fusion(f32[8192,64]{1,0:T(8,128)} %all-gather.8.cloned.1.call-done), kind=kOutput, calls=%fused_computation.64 | convolution fusion | flops 402653184 | bytes 2113536 | tf_op jit(solution)/shard_map/dot_general | solution.py:16
  331.1 5.8 cholesky.85
  338.3 4.9 custom-call.11
  345.8 5.8 cholesky.96
  353.0 4.9 custom-call.12
  358.8 5.9 cholesky.107
  366.0 4.9 custom-call.13
  370.9 2.8 copy.26
  374.1 107.1 %all-gather.14.cloned.1.call-done = bf16[8192,64]{1,0:T(8,128)(2,1)} async-done(((bf16[64,64]{1,0:T(8,128)(2,1)}), bf16[8192,64]{1,0:T(8,128)(2,1)}) %all-gather.14.cloned.1.call-update) | async-done | bytes 1048592 | tf_op jit(solution)/shard_map/all_gather | solution.py:37
  481.1 88.4 %all-gather.10.cloned.1.call-done = bf16[1,512,8192]{2,1,0:T(8,128)(2,1)} async-done(((bf16[1,128,8192]{2,1,0:T(8,128)(2,1)}), bf16[1,512,8192]{2,1,0:T(8,128)(2,1)}) %all-gather.10.cloned.1.call-update) | async-done | bytes 8388624 | tf_op jit(solution)/shard_map/all_gather | solution.py:33
  569.6 6.7 fusion.9
  576.9 139.4 %all-gather.12.cloned.1.call-done = bf16[8192,256]{1,0:T(8,128)(2,1)} async-done(((bf16[64,256]{1,0:T(8,128)(2,1)}), bf16[8192,256]{1,0:T(8,128)(2,1)}) %all-gather.12.cloned.1.call-update) | async-done | bytes 4194320 | tf_op jit(solution)/shard_map/all_gather | solution.py:36
  716.3 6.9 add_convert_fusion
  723.7 25.3 %while.26 = (s32[]{:T(128)}, f32[2,2]{1,0:T(2,128)S(1)}, bf16[2,8,512,128]{2,3,1,0:T(8,128)(2,1)}, bf16[2,2,512,128]{3,2,1,0:T(8,128)(2,1)S(1)}, s32[]{:T(128)},...) while((s32[]{:T(128)}, f32[2,2]{1,0:T(2,128)S(1)}, ...), condition=%wide.region_9.13_spmd.clone.clone, body=%wide.region_2.12_spmd.clone.clone.sunk | while | flops 138674192 | bytes 10113394 | solution.py:68
  723.7 1.3 constant_dynamic-slice_fusion.2
  725.8 10.4 %while.27 = (s32[]{:T(128)}, f32[8,2]{1,0:T(8,128)S(1)}, pred[512,512]{0,1:T(8,128)(4,1)S(1)}, bf16[8,512,128]{2,1,0:T(8,128)(2,1)S(1)}, bf16[2,512,128]{2,1,0:T(8,128)(2,1)S(1)}, /*index=5*/s32[]{:T(128)}, s32[]{:T(128)}) while((s32[]{:T(128)}, f32[8,2]{1,0:T(8,128)S(1)}, pred[512,512]{0,1:T(8,128)(4,1)S(1)}, ...), condition=%wide.region_7.10_spmd.clone, body=%wide.region_3.9_spmd.clone.sunk | while | flops 138412032 | bytes 5132397 | solution.py:65
  736.3 1.3 constant_dynamic-slice_fusion.2
  738.5 10.4 %while.27 = (s32[]{:T(128)}, f32[8,2]{1,0:T(8,128)S(1)}, pred[512,512]{0,1:T(8,128)(4,1)S(1)}, bf16[8,512,128]{2,1,0:T(8,128)(2,1)S(1)}, bf16[2,512,128]{2,1,0:T(8,128)(2,1)S(1)}, /*index=5*/s32[]{:T(128)}, s32[]{:T(128)}) while((s32[]{:T(128)}, f32[8,2]{1,0:T(8,128)S(1)}, pred[512,512]{0,1:T(8,128)(4,1)S(1)}, ...), condition=%wide.region_7.10_spmd.clone, body=%wide.region_3.9_spmd.clone.sunk | while | flops 138412032 | bytes 5132397 | solution.py:65
  750.1 101.5 %psum.7 = f32[2]{0:T(128)S(1)} all-reduce(f32[2]{0:T(128)S(1)} %reduce_sum.36), channel_id=1, replica_groups=mesh['fsdp'=128,'seq'=4] {'fsdp','seq'}, use_global_device_ids=true, to_apply=%region_11.15 | all-reduce | flops 2 | bytes 16 | tf_op jit(solution)/shard_map/psum | solution.py:69
  (128 shorter events, 36.2 us)
Async XLA Ops:
  7.2 338.2 %copy-start = (f32[1024,64]{0,1:T(8,128)S(1)}, f32[1024,64]{0,1:T(8,128)}, u32[]{:S(2)}) copy-start(f32[1024,64]{0,1:T(8,128)} %param.18) | copy-start | bytes 786436
  7.2 151.8 %all-gather.6.cloned.1.call-start = ((), (), s32[]{:S(2)}) async-start(), calls=%async_computation | async-start | bytes 4227072 | tf_op jit(solution)/shard_map/all_gather | solution.py:30
  7.9 173.7 %copy-start.2 = (f32[64,64]{1,0:T(8,128)S(1)}, f32[64,64]{1,0:T(8,128)}, u32[]{:S(2)}) copy-start(f32[64,64]{1,0:T(8,128)} %param.17) | copy-start | bytes 49156
  7.9 312.6 %all-gather.8.cloned.1.call-start = ((), (), s32[]{:S(2)}) async-start(), calls=%async_computation.1 | async-start | bytes 4227072 | tf_op jit(solution)/shard_map/all_gather | solution.py:30
  182.6 298.5 %all-gather.14.cloned.1.call-start = ((), (), s32[]{:S(2)}) async-start(), calls=%async_computation.4 | async-start | bytes 2113536 | tf_op jit(solution)/shard_map/all_gather | solution.py:37
  344.2 26.7 %copy-start.1 = (bf16[1,512,2048]{2,1,0:T(8,128)(2,1)S(1)}, bf16[1,512,2048]{2,1,0:T(8,128)(2,1)}, u32[]{:S(2)}) copy-start(bf16[1,512,2048]{2,1,0:T(8,128)(2,1)} %param.15) | copy-start | bytes 6291460
  344.2 225.4 %all-gather.10.cloned.1.call-start = ((), (), s32[]{:S(2)}) async-start(), calls=%async_computation.2 | async-start | bytes 10485760 | tf_op jit(solution)/shard_map/all_gather | solution.py:33
  344.7 371.6 %all-gather.12.cloned.1.call-start = ((), (), s32[]{:S(2)}) async-start(), calls=%async_computation.3 | async-start | bytes 4227072 | tf_op jit(solution)/shard_map/all_gather | solution.py:36
Sparse Core Ops, SparseCore 0:
  11.1 147.8 all-gather.5
  182.7 137.7 all-gather.7
  344.3 136.8 all-gather.13
  483.1 86.4 all-gather.9
  572.5 143.6 all-gather.11
where the time goes:
time: 859 us
  waiting for transfers between devices  625 us (73%)
  blocking collectives  101 us (12%)
  other arithmetic  60.3 us (7%)
  matrix products  47.2 us (5%)
  between operations  14 us (2%)
  local copies, waits for them, and re-layouts  9.49 us (1%)
    all_gather x2, waiting for transfers between devices, local(): whole_u = lax.all_gather(u_rows, 'fsdp', axis=0, tiled=True)  289 us
    all_gather x1, waiting for transfers between devices, local(): weight_piece = lax.all_gather(key_weight, 'fsdp', axis=0, tiled=True)  139 us
    all_gather x1, waiting for transfers between devices, local(): factor_piece = lax.all_gather(q_low, 'fsdp', axis=0, tiled=True)  107 us
    psum x1, blocking collectives, local(): sums = lax.psum(partial_sums, ('fsdp', 'seq'))  101 us
    all_gather x1, waiting for transfers between devices, local(): whole_x = lax.all_gather(tokens, 'seq', axis=1, tiled=True)[0]  88.4 us
    another operation x12, other arithmetic, solve_rows(): lower = jnp.linalg.cholesky(gram)  26.1 us
    dot_general x6, matrix products, highest(): jnp.dot(left, right, precision=lax.Precision.HIGHEST, preferred_element_t...  23.4 us
    another operation x8, other arithmetic, solve_rows(): lax.linalg.triangular_solve(lower, rows, left_side=False, lower=True, tra...  22.2 us
  transfers between devices with their start and end apart: 5, of which 5 were waited for; matrix products, arithmetic and copies ran while one was open for 4% of the time, Pallas kernels for 0%

commit v1 on v0

--- a/solution.py
+++ b/solution.py
@@ -10,6 +10,24 @@
 R = 64
 KD = 1024
 GROUP = 8
+
+
+def collect(array, axis, dim):
+    ways, here, step = (lax.axis_size(axis), lax.axis_index(axis), array.shape[dim])
+    dims = [n * ways if d == dim else n for d, n in enumerate(array.shape)]
+    full = lax.dynamic_update_slice_in_dim(
+        jnp.zeros(dims, array.dtype), array, here * step, axis=dim
+    )
+    going_up = going_down = array
+    for far in range(1, ways // 2 + 1):
+        going_up = lax.ppermute(going_up, axis, [(d, (d + 1) % ways) for d in range(ways)])
+        full = lax.dynamic_update_slice_in_dim(full, going_up, (here - far) % ways * step, axis=dim)
+        if 2 * far < ways:
+            going_down = lax.ppermute(going_down, axis, [(d, (d - 1) % ways) for d in range(ways)])
+            full = lax.dynamic_update_slice_in_dim(
+                full, going_down, (here + far) % ways * step, axis=dim
+            )
+    return full
 
 
 def highest(left, right):
@@ -30,7 +48,7 @@
         whole_u = lax.all_gather(u_rows, "fsdp", axis=0, tiled=True)
         u_rows = solve_rows(u_rows, highest(whole_u.T, whole_u))
     q_low = u_rows.astype(jnp.bfloat16)
-    whole_x = lax.all_gather(tokens, "seq", axis=1, tiled=True)[0]
+    whole_x = collect(tokens, "seq", 1)[0]
     length = whole_x.shape[0]
     slice_width = key_weight.shape[1]
     weight_piece = lax.all_gather(key_weight, "fsdp", axis=0, tiled=True)

time: 859 us -> 765 us (0.89)
  waiting for transfers between devices: 625 us -> 509 us
  local copies, waits for them, and re-layouts: 9.49 us -> 22.6 us
  starting transfers between devices: 0.38 us -> 9.23 us
    all_gather x1 -> x0, waiting for transfers between devices: 88.4 us -> none  [local(): whole_x = lax.all_gather(tokens, 'seq', axis=1, tiled=True)[0]]
    all_gather x1, waiting for transfers between devices: 107 us -> 35.5 us  [local(): factor_piece = lax.all_gather(q_low, 'fsdp', axis=0, tiled=True)]
    ppermute x0 -> x3, waiting for transfers between devices: none -> 50.2 us  [the longest x2 50.2 us: collect(): lax.ppermute(going_up, axis, [(d, (d + 1) % ways) for d in range(ways)])]
    dynamic_update_slice x0 -> x4, local copies, waits for them, and re-layouts: none -> 9.15 us  [the longest x2 4.59 us: collect(): lax.dynamic_update_slice_in_dim(full, going_up, (here - far) % ways * ste...]
    ppermute x0 -> x3, starting transfers between devices: none -> 8.89 us  [the longest x2 5.27 us: collect(): lax.ppermute(going_up, axis, [(d, (d + 1) % ways) for d in range(ways)])]
  transfers between devices with their start and end apart: 5 -> 7, of which waited for: 5 -> 6; matrix products, arithmetic and copies ran while one was open for 4% -> 6% of each run, Pallas kernels for 0% -> 0%
where the time goes in v1:
time: 765 us; the launch traced here: 764 us
  waiting for transfers between devices  509 us (67%)
  blocking collectives  101 us (13%)
  other arithmetic  60.3 us (8%)
  matrix products  47 us (6%)
  local copies, waits for them, and re-layouts  22.6 us (3%)
  between operations  14.1 us (2%)
  starting transfers between devices  9.23 us (1%)
    all_gather x2, waiting for transfers between devices, local(): whole_u = lax.all_gather(u_rows, 'fsdp', axis=0, tiled=True)  289 us
    all_gather x1, waiting for transfers between devices, local(): weight_piece = lax.all_gather(key_weight, 'fsdp', axis=0, tiled=True)  134 us
    psum x1, blocking collectives, local(): sums = lax.psum(partial_sums, ('fsdp', 'seq'))  101 us
    ppermute x2, waiting for transfers between devices, collect(): lax.ppermute(going_up, axis, [(d, (d + 1) % ways) for d in range(ways)])  50.2 us
    all_gather x1, waiting for transfers between devices, local(): factor_piece = lax.all_gather(q_low, 'fsdp', axis=0, tiled=True)  35.5 us
    another operation x12, other arithmetic, solve_rows(): lower = jnp.linalg.cholesky(gram)  26.1 us
    dot_general x6, matrix products, highest(): jnp.dot(left, right, precision=lax.Precision.HIGHEST, preferred_element_t...  23.3 us
    another operation x8, other arithmetic, solve_rows(): lax.linalg.triangular_solve(lower, rows, left_side=False, lower=True, tra...  22.2 us
  transfers between devices with their start and end apart: 7, of which 6 were waited for; matrix products, arithmetic and copies ran while one was open for 6% of the time, Pallas kernels for 0%

profile of v1, /device:TPU:1, one launch (start us, length us, event | category | flops | bytes accessed | tf_op | source)
XLA Modules:
  0.0 764.5 jit_solution(15409522878872433680)
XLA Ops:
  8.0 151.0 %all-gather.5.cloned.1.call-done = f32[8192,64]{1,0:T(8,128)} async-done(((f32[64,64]{1,0:T(8,128)}), f32[8192,64]{1,0:T(8,128)}) %all-gather.5.cloned.1.call-update) | async-done | bytes 2097168 | tf_op jit(solution)/shard_map/all_gather | solution.py:48
  159.0 10.4 %fusion.26 = f32[64,64]{1,0:T(8,128)S(1)} fusion(f32[8192,64]{1,0:T(8,128)} %all-gather.5.cloned.1.call-done), kind=kOutput, calls=%fused_computation.63 | convolution fusion | flops 402653184 | bytes 2113536 | tf_op jit(solution)/shard_map/dot_general | solution.py:34
  169.5 5.8 cholesky.74
  176.7 4.9 custom-call.10
  182.8 137.7 %all-gather.7.cloned.1.call-done = f32[8192,64]{1,0:T(8,128)} async-done(((f32[64,64]{1,0:T(8,128)}), f32[8192,64]{1,0:T(8,128)}) %all-gather.7.cloned.1.call-update) | async-done | bytes 2097168 | tf_op jit(solution)/shard_map/all_gather | solution.py:48
  320.6 10.4 %fusion.27 = f32[64,64]{1,0:T(8,128)S(1)} fusion(f32[8192,64]{1,0:T(8,128)} %all-gather.7.cloned.1.call-done), kind=kOutput, calls=%fused_computation.64 | convolution fusion | flops 402653184 | bytes 2113536 | tf_op jit(solution)/shard_map/dot_general | solution.py:34
  331.1 5.8 cholesky.85
  338.3 4.9 custom-call.11
  347.3 3.6 collective-permute-start.1
  351.5 5.8 cholesky.96
  358.7 4.9 custom-call.12
  364.5 5.9 cholesky.107
  371.7 4.9 custom-call.13
  379.1 4.2 squeeze.23
  385.3 9.3 %collective-permute-done = bf16[1,128,8192]{2,1,0:T(8,128)(2,1)} collective-permute-done((bf16[1,128,8192]{2,1,0:T(8,128)(2,1)}, bf16[1,128,8192]{2,1,0:T(8,128)(2,1)}, u32[]{:S(2)}, u32[]{:S(2)}) %collective-permute-start) | collective-permute-done | bytes 2097184 | tf_op jit(solution)/shard_map/ppermute | solution.py:23
  402.9 41.0 %collective-permute-done.2 = bf16[1,128,8192]{2,1,0:T(8,128)(2,1)S(1)} collective-permute-done((bf16[1,128,8192]{2,1,0:T(8,128)(2,1)}, bf16[1,128,8192]{2,1,0:T(8,128)(2,1)S(1)}, u32[]{:S(2)}, u32[]{:S(2)}) %collective-permute-start.2) | collective-permute-done | bytes 2097184 | tf_op jit(solution)/shard_map/ppermute | solution.py:23
  445.3 35.5 %all-gather.11.cloned.1.call-done = bf16[8192,64]{1,0:T(8,128)(2,1)} async-done(((bf16[64,64]{1,0:T(8,128)(2,1)}), bf16[8192,64]{1,0:T(8,128)(2,1)}) %all-gather.11.cloned.1.call-update) | async-done | bytes 1048592 | tf_op jit(solution)/shard_map/all_gather | solution.py:55
  480.9 6.6 fusion.30
  488.1 134.1 %all-gather.9.cloned.1.call-done = bf16[8192,256]{1,0:T(8,128)(2,1)} async-done(((bf16[64,256]{1,0:T(8,128)(2,1)}), bf16[8192,256]{1,0:T(8,128)(2,1)}) %all-gather.9.cloned.1.call-update) | async-done | bytes 4194320 | tf_op jit(solution)/shard_map/all_gather | solution.py:54
  622.3 6.9 add_convert_fusion
  629.6 25.2 %while.26 = (s32[]{:T(128)}, f32[2,2]{1,0:T(2,128)S(1)}, bf16[2,8,512,128]{2,3,1,0:T(8,128)(2,1)}, bf16[2,2,512,128]{3,2,1,0:T(8,128)(2,1)S(1)}, s32[]{:T(128)},...) while((s32[]{:T(128)}, f32[2,2]{1,0:T(2,128)S(1)}, ...), condition=%wide.region_9.13_spmd.clone.clone, body=%wide.region_2.12_spmd.clone.clone.sunk | while | flops 138674192 | bytes 10113394 | solution.py:86
  631.8 10.4 %while.27 = (s32[]{:T(128)}, f32[8,2]{1,0:T(8,128)S(1)}, pred[512,512]{0,1:T(8,128)(4,1)S(1)}, bf16[8,512,128]{2,1,0:T(8,128)(2,1)S(1)}, bf16[2,512,128]{2,1,0:T(8,128)(2,1)S(1)}, /*index=5*/s32[]{:T(128)}, s32[]{:T(128)}) while((s32[]{:T(128)}, f32[8,2]{1,0:T(8,128)S(1)}, pred[512,512]{0,1:T(8,128)(4,1)S(1)}, ...), condition=%wide.region_7.10_spmd.clone, body=%wide.region_3.0_spmd.clone.sunk | while | flops 138412032 | bytes 5132397 | solution.py:83
  644.4 10.4 %while.27 = (s32[]{:T(128)}, f32[8,2]{1,0:T(8,128)S(1)}, pred[512,512]{0,1:T(8,128)(4,1)S(1)}, bf16[8,512,128]{2,1,0:T(8,128)(2,1)S(1)}, bf16[2,512,128]{2,1,0:T(8,128)(2,1)S(1)}, /*index=5*/s32[]{:T(128)}, s32[]{:T(128)}) while((s32[]{:T(128)}, f32[8,2]{1,0:T(8,128)S(1)}, pred[512,512]{0,1:T(8,128)(4,1)S(1)}, ...), condition=%wide.region_7.10_spmd.clone, body=%wide.region_3.0_spmd.clone.sunk | while | flops 138412032 | bytes 5132397 | solution.py:83
  655.9 101.5 %psum.7 = f32[2]{0:T(128)S(1)} all-reduce(f32[2]{0:T(128)S(1)} %reduce_sum.36), channel_id=1, replica_groups=mesh['fsdp'=128,'seq'=4] {'fsdp','seq'}, use_global_device_ids=true, to_apply=%region_11.15 | all-reduce | flops 2 | bytes 16 | tf_op jit(solution)/shard_map/psum | solution.py:87
  (138 shorter events, 54.6 us)
Async XLA Ops:
  7.2 343.9 %copy-start = (f32[1024,64]{0,1:T(8,128)S(1)}, f32[1024,64]{0,1:T(8,128)}, u32[]{:S(2)}) copy-start(f32[1024,64]{0,1:T(8,128)} %param.18) | copy-start | bytes 786436
  7.2 151.8 %all-gather.5.cloned.1.call-start = ((), (), s32[]{:S(2)}) async-start(), calls=%async_computation | async-start | bytes 4227072 | tf_op jit(solution)/shard_map/all_gather | solution.py:48
  7.9 173.7 %copy-start.3 = (f32[64,64]{1,0:T(8,128)S(1)}, f32[64,64]{1,0:T(8,128)}, u32[]{:S(2)}) copy-start(f32[64,64]{1,0:T(8,128)} %param.17) | copy-start | bytes 49156
  7.9 312.6 %all-gather.7.cloned.1.call-start = ((), (), s32[]{:S(2)}) async-start(), calls=%async_computation.1 | async-start | bytes 4227072 | tf_op jit(solution)/shard_map/all_gather | solution.py:48
  182.6 194.0 %copy-start.1 = (bf16[1,512,2048]{2,1,0:T(8,128)(2,1)S(1)}, bf16[1,512,2048]{2,1,0:T(8,128)(2,1)}, u32[]{:S(2)}) copy-start(bf16[1,512,2048]{2,1,0:T(8,128)(2,1)} %param.15) | copy-start | bytes 6291460
  182.6 298.2 %all-gather.11.cloned.1.call-start = ((), (), s32[]{:S(2)}) async-start(), calls=%async_computation.3 | async-start | bytes 2113536 | tf_op jit(solution)/shard_map/all_gather | solution.py:55
  344.2 278.1 %all-gather.9.cloned.1.call-start = ((), (), s32[]{:S(2)}) async-start(), calls=%async_computation.2 | async-start | bytes 4227072 | tf_op jit(solution)/shard_map/all_gather | solution.py:54
  344.2 50.3 %collective-permute-start = (bf16[1,128,8192]{2,1,0:T(8,128)(2,1)}, bf16[1,128,8192]{2,1,0:T(8,128)(2,1)}, u32[]{:S(2)}, u32[]{:S(2)}) collective-permute-start(bf16[1,128,8192]{2,1,0:T(8,128)(2,1)} %param.14), channel_id=1, source_target_pairs={{0,1},{1,2},{2,3},{3,0},{4,5},{5,6},{6,7},{7,4},{8,9},{9,10},{10,1... | collective-permute-start | bytes 6291464 | tf_op jit(solution)/shard_map/ppermute | solution.py:23
  347.3 52.5 %collective-permute-start.1 = (bf16[1,128,8192]{2,1,0:T(8,128)(2,1)}, bf16[1,128,8192]{2,1,0:T(8,128)(2,1)}, u32[]{:S(2)}, u32[]{:S(2)}) collective-permute-start(bf16[1,128,8192]{2,1,0:T(8,128)(2,1)} %param.14), channel_id=1, source_target_pairs={{0,3},{1,0},{2,1},{3,2},{4,7},{5,4},{6,5},{7,6},{8,11},{9,8},{10,9... | collective-permute-start | bytes 6291464 | tf_op jit(solution)/shard_map/ppermute | solution.py:26
  379.1 4.2 copy-start.2
  394.5 49.4 %collective-permute-start.2 = (bf16[1,128,8192]{2,1,0:T(8,128)(2,1)}, bf16[1,128,8192]{2,1,0:T(8,128)(2,1)S(1)}, u32[]{:S(2)}, u32[]{:S(2)}) collective-permute-start(bf16[1,128,8192]{2,1,0:T(8,128)(2,1)} %collective-permute-done), channel_id=1, source_target_pairs={{0,1},{1,2},{2,3},{3,0},{4,5},{5,6},{6,7},{7,4},{8,9},{9,10},{10,1... | collective-permute-start | bytes 6291464 | tf_op jit(solution)/shard_map/ppermute | solution.py:23
Sparse Core Ops, SparseCore 0:
  11.1 147.8 all-gather.4
  182.7 137.7 all-gather.6
  344.3 136.5 all-gather.10
  483.9 138.3 all-gather.8
